TPU v7x, 256 devices: a whole 4x4x8 slice. The times are simulated.
256 devices in a mesh: row: 32 (over z, x), col: 8 (over y, core).
Axes of the slice: x: 4, y: 4, z: 8, core: 2. Of those that a mesh axis runs over, the one named last changes fastest.
Arguments:
- tokens: bfloat16 [1024, 8192], P('row', 'col'), may hold values from -6 to 6
- cotangent: bfloat16 [1024, 8192], P('row', 'col'), may hold values from -6 to 6
- gate_weight: bfloat16 [8192, 16384], P('col', 'row'), may hold values from -0.125 to 0.125
- up_weight: bfloat16 [8192, 16384], P('col', 'row'), may hold values from -0.125 to 0.125
- down_weight: bfloat16 [16384, 8192], P('row', 'col'), may hold values from -0.078125 to 0.078125
- gate_mask: int32 [64, 128], P('col', 'row'), may hold values 0 or 1
- up_mask: int32 [64, 128], P('col', 'row'), may hold values 0 or 1
- down_mask: int32 [128, 64], P('row', 'col'), may hold values 0 or 1
Outputs:
- layer_out: bfloat16 [1024, 8192], P('row', 'col')
- grad_tokens: bfloat16 [1024, 8192], P('row', 'col')
- grad_gate_weight: float32 [8192, 16384], P('col', 'row')
- grad_up_weight: float32 [8192, 16384], P('col', 'row')
- grad_down_weight: float32 [16384, 8192], P('row', 'col')
All inputs are finite; a program needn't handle non-finite values. No bound on the sum of `gate_mask` or of `up_mask` or of `down_mask` on one device may be relied on, other than what follows from the above.
Results may differ from a plain program's by a relative error of at most 0.0049.
Values may be sent and summed in bfloat16 or wider, within the bound.
No kernel may reach another device: no remote copies, remote signals or barrier semaphores. Data moves between devices by JAX's collectives and lax.ppermute only.
A program may use at most 128 MiB of HBM per device.

v0:
```python
import jax
import jax.numpy as jnp
from jax import lax
from jax.sharding import PartitionSpec as P

BLOCK = 128
contract_inner = (((1,), (1,)), ((), ()))
contract_outer = (((0,), (0,)), ((), ()))


def apply_pattern(weight, pattern):
    row_blocks, col_blocks = pattern.shape
    block_scale = pattern.astype(weight.dtype)
    blocks = weight.reshape(row_blocks, BLOCK, col_blocks, BLOCK) * block_scale[:, None, :, None]
    return blocks.reshape(weight.shape)


def col_reduce(summands, finish):
    summed = lax.psum(summands, "col")
    return finish(summed)


def shards(tokens, cotangent, gate_weight, up_weight, down_weight, gate_mask, up_mask, down_mask):
    hidden_width = gate_weight.shape[1]
    gathered_tokens, gathered_grads = (
        lax.all_gather(tokens, "row", axis=0, tiled=True),
        lax.all_gather(cotangent, "row", axis=0, tiled=True),
    )
    joint_weight = jnp.concatenate(
        [apply_pattern(gate_weight, gate_mask), apply_pattern(up_weight, up_mask)], axis=1
    )
    masked_down = apply_pattern(down_weight, down_mask)
    joint_part = jnp.dot(gathered_tokens, joint_weight, preferred_element_type=jnp.float32)

    def activate(joint_pre):
        gate_pre = joint_pre[:, :hidden_width]
        up_pre = joint_pre[:, hidden_width:]
        hidden_rows = (gate_pre * jax.nn.sigmoid(gate_pre) * up_pre).astype(jnp.bfloat16)
        return (hidden_rows, joint_pre)

    hidden, joint_pre = col_reduce(joint_part, activate)
    hidden_part = lax.dot_general(
        gathered_grads, masked_down, contract_inner, preferred_element_type=jnp.float32
    )

    def derive(grad_hidden):
        gate_pre = joint_pre[:, :hidden_width]
        up_pre = joint_pre[:, hidden_width:]
        sigmoid_gate = jax.nn.sigmoid(gate_pre)
        silu_gate = gate_pre * sigmoid_gate
        grad_gate_pre = (
            grad_hidden * up_pre * sigmoid_gate * (1.0 + gate_pre * (1.0 - sigmoid_gate))
        )
        grad_up_pre = grad_hidden * silu_gate
        joint_rows = jnp.concatenate(
            [grad_gate_pre.astype(jnp.bfloat16), grad_up_pre.astype(jnp.bfloat16)], axis=1
        )
        return (joint_rows, grad_hidden)

    joint_grad, unused = col_reduce(hidden_part, derive)
    output_term = jnp.dot(hidden, masked_down, preferred_element_type=jnp.float32)
    token_term = lax.dot_general(
        joint_grad, joint_weight, contract_inner, preferred_element_type=jnp.float32
    )
    layer_out, grad_tokens = (
        lax.psum_scatter(output_term, "row", scatter_dimension=0, tiled=True),
        lax.psum_scatter(token_term, "row", scatter_dimension=0, tiled=True),
    )
    weight_grads = lax.dot_general(
        gathered_tokens, joint_grad, contract_outer, preferred_element_type=jnp.float32
    )
    grad_gate_weight = apply_pattern(weight_grads[:, :hidden_width], gate_mask)
    grad_up_weight = apply_pattern(weight_grads[:, hidden_width:], up_mask)
    grad_down_weight = apply_pattern(
        lax.dot_general(hidden, gathered_grads, contract_outer, preferred_element_type=jnp.float32),
        down_mask,
    )
    return (
        layer_out.astype(jnp.bfloat16),
        grad_tokens.astype(jnp.bfloat16),
        grad_gate_weight,
        grad_up_weight,
        grad_down_weight,
    )


def solution(mesh):
    in_specs = (
        P("row", "col"),
        P("row", "col"),
        P("col", "row"),
        P("col", "row"),
        P("row", "col"),
        P("col", "row"),
        P("col", "row"),
        P("row", "col"),
    )
    out_specs = (
        P("row", "col"),
        P("row", "col"),
        P("col", "row"),
        P("col", "row"),
        P("row", "col"),
    )
    return jax.shard_map(shards, mesh=mesh, in_specs=in_specs, out_specs=out_specs, check_vma=False)
```

profile of v0, /device:TPU:8, one launch (start us, length us, event | category | flops | bytes accessed | tf_op | source)
XLA Modules:
  0.0 727.5 jit_solution(3877633077299212398)
XLA Ops:
  8.7 0.8 fusion.8
  9.6 0.8 fusion.7
  10.4 0.8 fusion.6
  11.9 1.3 bitcast_multiply_fusion.4
  13.2 78.2 %all-gather.3.cloned.1.call-done = bf16[1024,1024]{1,0:T(8,128)(2,1)} async-done(((bf16[32,1024]{1,0:T(8,128)(2,1)}), bf16[1024,1024]{1,0:T(8,128)(2,1)}) %all-gather.3.cloned.1.call-update) | async-done | bytes 2097168 | tf_op jit(solution)/shard_map/all_gather | solution.py:26
  91.4 6.4 convolution_bitcast_fusion.1
  97.8 71.4 %all-gather.5.cloned.1.call-done = bf16[1024,1024]{1,0:T(8,128)(2,1)} async-done(((bf16[32,1024]{1,0:T(8,128)(2,1)}), bf16[1024,1024]{1,0:T(8,128)(2,1)}) %all-gather.5.cloned.1.call-update) | async-done | bytes 2097168 | tf_op jit(solution)/shard_map/all_gather | solution.py:27
  169.4 4.2 convolution_bitcast_fusion.2
  173.7 84.3 %all-reduce.3.cloned.1.call-done = (f32[1024,1024]{0,1:T(8,128)}, f32[1024,512]{0,1:T(8,128)}) async-done(((f32[1024,1024]{0,1:T(8,128)}, f32[1024,512]{0,1:T(8,128)}), (f32[1024,1024]{0,1:T(8,128)}, f32[1024,512]{0,1:T(8,128)})) %all-reduce.3.cloned.1.call-update) | async-done | bytes 6291472 | tf_op jit(solution)/shard_map/psum | solution.py:19
  258.0 4.4 multiply_convert_fusion.1
  262.4 1.0 copy-done.1
  263.7 4.4 fusion.1
  268.3 3.3 fusion.2
  271.6 1.2 copy-done.2
  273.1 3.9 convolution_bitcast_fusion
  277.4 2.8 bitcast_multiply_fusion.1
  280.3 2.9 copy.15
  283.2 1.8 copy.16
  285.2 1.4 copy-done.10
  286.6 2.7 bitcast_multiply_fusion
  289.3 204.7 %reduce-scatter.5.cloned.1.call-done = f32[32,1024]{1,0:T(8,128)} async-done(((f32[1024,1024]{1,0:T(8,128)}), f32[32,1024]{1,0:T(8,128)}) %reduce-scatter.5.cloned.1.call-update) | async-done | bytes 131088 | tf_op jit(solution)/shard_map/reduce_scatter | solution.py:67
  494.0 1.5 convert_element_type.40
  495.5 223.9 %reduce-scatter.3.cloned.1.call-done = f32[32,1024]{1,0:T(8,128)} async-done(((f32[1024,1024]{1,0:T(8,128)}), f32[32,1024]{1,0:T(8,128)}) %reduce-scatter.3.cloned.1.call-update) | async-done | bytes 131088 | tf_op jit(solution)/shard_map/reduce_scatter | solution.py:66
  719.5 1.5 convert_element_type.37
  (37 shorter events, 4.1 us)
Async XLA Ops:
  7.2 4.7 copy-start.6
  7.2 4.7 copy-start.5
  7.2 84.2 %all-gather.3.cloned.1.call-start = ((), (), s32[]{:S(2)}) async-start(), calls=%async_computation.2 | async-start | bytes 2162688 | tf_op jit(solution)/shard_map/all_gather | solution.py:26
  7.9 161.2 %all-gather.5.cloned.1.call-start = ((), (), s32[]{:S(2)}) async-start(), calls=%async_computation.4 | async-start | bytes 2162688 | tf_op jit(solution)/shard_map/all_gather | solution.py:27
  8.7 249.3 %all-reduce.3.cloned.1.call-start = ((), (), s32[]{:S(2)}) async-start(), calls=%async_computation.6 | async-start | bytes 12582912 | tf_op jit(solution)/shard_map/psum | solution.py:19
  13.2 84.6 %copy-start.7 = (bf16[1024,512]{1,0:T(8,128)(2,1)}, bf16[1024,512]{1,0:T(8,128)(2,1)S(1)}, u32[]{:S(2)}) copy-start(bf16[1024,512]{1,0:T(8,128)(2,1)S(1)} %get-tuple-element.23) | copy-start | bytes 3145732
  91.4 78.0 %copy-start = (bf16[512,1024]{1,0:T(8,128)(2,1)S(1)}, bf16[512,1024]{1,0:T(8,128)(2,1)}, u32[]{:S(2)}) copy-start(bf16[512,1024]{1,0:T(8,128)(2,1)} %param.12) | copy-start | bytes 3145732
  173.6 320.4 %reduce-scatter.5.cloned.1.call-start = ((), (), s32[]{:S(2)}) async-start(), calls=%async_computation.5 | async-start | bytes 4325376 | tf_op jit(solution)/shard_map/reduce_scatter | solution.py:67
  258.0 5.7 copy-start.8
  258.0 5.7 copy-start.9
  262.3 1.0 copy-start.1
  262.4 1.3 copy-start.3
  268.1 451.4 %reduce-scatter.3.cloned.1.call-start = ((), (), s32[]{:S(2)}) async-start(), calls=%async_computation.3 | async-start | bytes 4325376 | tf_op jit(solution)/shard_map/reduce_scatter | solution.py:66
  271.6 1.2 copy-start.2
  271.6 1.5 copy-start.4
  285.0 1.6 copy-start.10
Sparse Core Ops, SparseCore 0:
  10.6 80.7 all-gather.2
  94.0 75.1 all-gather.4
  173.7 84.1 all-reduce.2
  268.2 225.7 reduce-scatter.4
  497.7 221.6 reduce-scatter.2
where the time goes:
time: 728 us
  waiting for transfers between devices  664 us (91%)
  matrix products  24.9 us (3%)
  other arithmetic  13.9 us (2%)
  between operations  13.9 us (2%)
  local copies, waits for them, and re-layouts  10.6 us (1%)
    reduce_scatter x1, waiting for transfers between devices, shards(): lax.psum_scatter(output_term, 'row', scatter_dimension=0, tiled=True)  224 us
    reduce_scatter x1, waiting for transfers between devices, shards(): lax.psum_scatter(token_term, 'row', scatter_dimension=0, tiled=True)  205 us
    psum x1, waiting for transfers between devices, col_reduce(): summed = lax.psum(summands, 'col')  84.3 us
    all_gather x1, waiting for transfers between devices, shards(): lax.all_gather(tokens, 'row', axis=0, tiled=True)  78.2 us
    all_gather x1, waiting for transfers between devices, shards(): lax.all_gather(cotangent, 'row', axis=0, tiled=True)  71.4 us
  transfers between devices with their start and end apart: 5, of which 5 were waited for; matrix products, arithmetic and copies ran while one was open for 4% of the time, Pallas kernels for 0%

commit v1 on v0

--- a/solution.py
+++ b/solution.py
@@ -16,7 +16,7 @@
 
 
 def col_reduce(summands, finish):
-    summed = lax.psum(summands, "col")
+    summed = jnp.sum(lax.all_gather(summands, "col"), axis=0)
     return finish(summed)
 
 

time: 728 us -> 934 us (1.28)
  waiting for transfers between devices: 664 us -> 794 us
  local copies, waits for them, and re-layouts: 10.6 us -> 68.2 us
  other arithmetic: 13.9 us -> 31.6 us
    all_gather x0 -> x2, waiting for transfers between devices: none -> 215 us  [col_reduce(): summed = jnp.sum(lax.all_gather(summands, 'col'), axis=0)]
    psum x1 -> x0, waiting for transfers between devices: 84.3 us -> none  [col_reduce(): summed = lax.psum(summands, 'col')]
    unnamed x24 -> x34, local copies, waits for them, and re-layouts: 8.91 us -> 66.5 us
    reduce_sum x0 -> x2, other arithmetic: none -> 19.2 us  [col_reduce(): summed = jnp.sum(lax.all_gather(summands, 'col'), axis=0)]
    all_gather x1, waiting for transfers between devices: 71.4 us -> 81.9 us  [shards(): lax.all_gather(cotangent, 'row', axis=0, tiled=True)]
  transfers between devices with their start and end apart: 5 -> 6, of which waited for: 5 -> 6; matrix products, arithmetic and copies ran while one was open for 4% -> 6% of each run, Pallas kernels for 0% -> 0%
where the time goes in v1:
time: 934 us; the launch traced here: 933 us
  waiting for transfers between devices  794 us (85%)
  local copies, waits for them, and re-layouts  68.2 us (7%)
  other arithmetic  31.6 us (3%)
  matrix products  25.2 us (3%)
  between operations  14.2 us (2%)
    reduce_scatter x1, waiting for transfers between devices, shards(): lax.psum_scatter(output_term, 'row', scatter_dimension=0, tiled=True)  224 us
    all_gather x2, waiting for transfers between devices, col_reduce(): summed = jnp.sum(lax.all_gather(summands, 'col'), axis=0)  215 us
    reduce_scatter x1, waiting for transfers between devices, shards(): lax.psum_scatter(token_term, 'row', scatter_dimension=0, tiled=True)  202 us
    all_gather x1, waiting for transfers between devices, shards(): lax.all_gather(cotangent, 'row', axis=0, tiled=True)  81.9 us
    all_gather x1, waiting for transfers between devices, shards(): lax.all_gather(tokens, 'row', axis=0, tiled=True)  69.2 us
    unnamed x34, local copies, waits for them, and re-layouts  66.5 us
    reduce_sum x2, other arithmetic, col_reduce(): summed = jnp.sum(lax.all_gather(summands, 'col'), axis=0)  19.2 us
  transfers between devices with their start and end apart: 6, of which 6 were waited for; matrix products, arithmetic and copies ran while one was open for 6% of the time, Pallas kernels for 0%

profile of v1, /device:TPU:8, one launch (start us, length us, event | category | flops | bytes accessed | tf_op | source)
XLA Modules:
  0.0 933.4 jit_solution(16355615271312193441)
XLA Ops:
  9.5 81.9 %all-gather.9.cloned.1.call-done = bf16[1024,1024]{1,0:T(8,128)(2,1)} async-done(((bf16[32,1024]{1,0:T(8,128)(2,1)}), bf16[1024,1024]{1,0:T(8,128)(2,1)}) %all-gather.9.cloned.1.call-update) | async-done | bytes 2097168 | tf_op jit(solution)/shard_map/all_gather | solution.py:27
  92.6 4.5 convolution_bitcast_fusion.2
  98.7 1.3 bitcast_multiply_fusion.4
  100.0 69.2 %all-gather.7.cloned.1.call-done = bf16[1024,1024]{1,0:T(8,128)(2,1)} async-done(((bf16[32,1024]{1,0:T(8,128)(2,1)}), bf16[1024,1024]{1,0:T(8,128)(2,1)}) %all-gather.7.cloned.1.call-update) | async-done | bytes 2097168 | tf_op jit(solution)/shard_map/all_gather | solution.py:26
  169.1 6.4 convolution_bitcast_fusion.1
  175.8 80.1 %all-gather.13.cloned.1.call-done = f32[8192,512]{0,1:T(8,128)} async-done(((f32[1024,512]{0,1:T(8,128)}), f32[8192,512]{0,1:T(8,128)}) %all-gather.13.cloned.1.call-update) | async-done | bytes 16777232 | tf_op jit(solution)/shard_map/all_gather | solution.py:19
  255.9 19.7 %copy.25 = f32[64,8,8,1024]{3,2,1,0:T(8,128)S(1)} copy(f32[64,8,8,1024]{3,1,2,0:T(8,128)} %bitcast.53) | data formatting | bytes 33554432
  275.6 6.6 bitcast_reduce_fusion.1
  282.2 134.8 %all-gather.11.cloned.1.call-done = f32[8192,1024]{0,1:T(8,128)} async-done(((f32[1024,1024]{0,1:T(8,128)}), f32[8192,1024]{0,1:T(8,128)}) %all-gather.11.cloned.1.call-update) | async-done | bytes 33554448 | tf_op jit(solution)/shard_map/all_gather | solution.py:19
  417.1 34.9 %copy.23 = f32[128,8,8,1024]{3,2,1,0:T(8,128)S(1)} copy(f32[128,8,8,1024]{3,1,2,0:T(8,128)} %bitcast.52) | data formatting | bytes 67108864
  452.0 12.6 %bitcast_reduce_fusion = f32[1024,1024]{0,1:T(8,128)} fusion(f32[128,8,8,1024]{3,2,1,0:T(8,128)S(1)} %copy.23), kind=kLoop, calls=%fused_computation | loop fusion | flops 7340032 | bytes 37748736 | tf_op jit(solution)/shard_map/reduce_sum | solution.py:19
  464.5 4.4 multiply_convert_fusion.1
  470.2 4.4 fusion.1
  476.2 3.2 fusion.2
  481.0 3.9 convolution_bitcast_fusion
  485.3 2.8 bitcast_multiply_fusion.1
  488.2 2.9 copy.19
  491.0 1.8 copy.20
  493.1 1.4 copy-done.14
  494.5 2.7 bitcast_multiply_fusion
  497.2 202.2 %reduce-scatter.5.cloned.1.call-done = f32[32,1024]{1,0:T(8,128)} async-done(((f32[1024,1024]{1,0:T(8,128)}), f32[32,1024]{1,0:T(8,128)}) %reduce-scatter.5.cloned.1.call-update) | async-done | bytes 131088 | tf_op jit(solution)/shard_map/reduce_scatter | solution.py:67
  699.4 1.5 convert_element_type.40
  701.0 224.1 %reduce-scatter.3.cloned.1.call-done = f32[32,1024]{1,0:T(8,128)} async-done(((f32[1024,1024]{1,0:T(8,128)}), f32[32,1024]{1,0:T(8,128)}) %reduce-scatter.3.cloned.1.call-update) | async-done | bytes 131088 | tf_op jit(solution)/shard_map/reduce_scatter | solution.py:66
  925.0 1.5 convert_element_type.37
  (52 shorter events, 10.2 us)
Async XLA Ops:
  7.2 84.2 %all-gather.9.cloned.1.call-start = ((), (), s32[]{:S(2)}) async-start(), calls=%async_computation.4 | async-start | bytes 2162688 | tf_op jit(solution)/shard_map/all_gather | solution.py:27
  7.9 161.2 %all-gather.7.cloned.1.call-start = ((), (), s32[]{:S(2)}) async-start(), calls=%async_computation.2 | async-start | bytes 2162688 | tf_op jit(solution)/shard_map/all_gather | solution.py:26
  8.6 247.3 %all-gather.13.cloned.1.call-start = ((), (), s32[]{:S(2)}) async-start(), calls=%async_computation.7 | async-start | bytes 18874368 | tf_op jit(solution)/shard_map/all_gather | solution.py:19
  91.6 1.0 copy-start
  97.1 0.7 copy-start.12
  97.1 0.8 copy-start.13
  97.1 1.6 copy-start.7
  97.1 1.6 copy-start.8
  97.1 319.9 %all-gather.11.cloned.1.call-start = ((), (), s32[]{:S(2)}) async-start(), calls=%async_computation.6 | async-start | bytes 37748736 | tf_op jit(solution)/shard_map/all_gather | solution.py:19
  100.0 75.5 %copy-start.9 = (bf16[1024,512]{1,0:T(8,128)(2,1)}, bf16[1024,512]{1,0:T(8,128)(2,1)S(1)}, u32[]{:S(2)}) copy-start(bf16[1024,512]{1,0:T(8,128)(2,1)S(1)} %get-tuple-element.26) | copy-start | bytes 3145732
  175.5 523.9 %reduce-scatter.5.cloned.1.call-start = ((), (), s32[]{:S(2)}) async-start(), calls=%async_computation.5 | async-start | bytes 4325376 | tf_op jit(solution)/shard_map/reduce_scatter | solution.py:67
  464.5 5.7 copy-start.10
  464.5 5.7 copy-start.11
  468.9 1.1 copy-start.3
  468.9 1.3 copy-start.5
  474.6 1.2 copy-start.1
  474.6 1.5 copy-start.2
  474.7 450.3 %reduce-scatter.3.cloned.1.call-start = ((), (), s32[]{:S(2)}) async-start(), calls=%async_computation.3 | async-start | bytes 4325376 | tf_op jit(solution)/shard_map/reduce_scatter | solution.py:66
  479.4 1.2 copy-start.4
  479.4 1.5 copy-start.6
  492.9 1.6 copy-start.14
Sparse Core Ops, SparseCore 0:
  10.6 80.7 all-gather.8
  94.0 75.1 all-gather.6
  171.6 84.3 all-gather.12
  257.6 159.4 all-gather.10
  474.8 224.5 reduce-scatter.4
  703.2 221.8 reduce-scatter.2
